TPU v7x, 128 devices: a whole 4x4x4 slice. The times are simulated.
128 devices in a mesh: dp: 32 (over y, z_lo, x), tensor: 4 (over z_hi, core).
Axes of the slice: x: 4, y: 4, z: 4 (z_hi: 2, z_lo: 2; z = z_hi * 2 + z_lo), core: 2. Of those that a mesh axis runs over, the one named last changes fastest.
Arguments:
- tokens: bfloat16 [32768, 4096], P('dp'), may hold values from -6 to 6
- grad_out: bfloat16 [32768, 2048], P('dp', 'tensor'), may hold values from -12 to 12
- w_query: bfloat16 [4096, 2048], P('dp', 'tensor'), may hold values from -2 to 2
- w_key: bfloat16 [4096, 512], P('dp', 'tensor'), may hold values from -2 to 2
- value_matrix: bfloat16 [4096, 512], P('dp', 'tensor'), may hold values from -0.09375 to 0.09375
Outputs:
- grad_tokens: bfloat16 [32768, 4096], P('dp', 'tensor')
- grad_query: bfloat16 [4096, 2048], P('dp', 'tensor')
- grad_key: bfloat16 [4096, 512], P('dp', 'tensor')
- grad_value: bfloat16 [4096, 512], P('dp', 'tensor')
All inputs are finite; a program needn't handle non-finite values.
Results may differ from a plain program's by a relative error of at most 0.03.
The roundings to bfloat16 on the way count: a program that leaves them out, or rounds other values in their place, can miss the bound.
Values may be sent and summed in bfloat16 or wider, within the bound.
No kernel may reach another device: no remote copies, remote signals or barrier semaphores. Data moves between devices by JAX's collectives and lax.ppermute only.
A program may use at most 192 MiB of HBM per device.

v0:
```python
import jax
import jax.numpy as jnp
from jax import lax
from jax.sharding import Mesh
from jax.sharding import PartitionSpec as P

MODEL_WIDTH = 4096
HEAD_SIZE = 128
rope_base = 500000.0


def position_tables(length, head_dim):
    half_dim = head_dim // 2
    positions = jnp.arange(length, dtype=jnp.float32)
    inverse = jnp.power(
        jnp.float32(rope_base), -2.0 * jnp.arange(half_dim, dtype=jnp.float32) / head_dim
    )
    angles = positions[:, None] * inverse[None, :]
    cosine = jnp.concatenate([jnp.cos(angles), jnp.cos(angles)], axis=-1)[:, None, :]
    sine_table = jnp.concatenate([jnp.sin(angles), jnp.sin(angles)], axis=-1)[:, None, :]
    return (cosine, sine_table)


def half_turn(values):
    lower, upper = jnp.split(values, 2, axis=-1)
    return jnp.concatenate([-upper, lower], axis=-1)


def rotate_forward(values, cosine, sine_table):
    return values * cosine + half_turn(values) * sine_table


def rotate_back(grads, cosine, sine_table):
    return grads * cosine - half_turn(grads * sine_table)


def attention_backward(unrotated_query, unrotated_key, projected_value, upstream_flat, kv_heads):
    length = unrotated_query.shape[0]
    heads = unrotated_query.shape[1] // HEAD_SIZE
    group_size = heads // kv_heads
    cosine, sine_table = position_tables(length, HEAD_SIZE)
    query = rotate_forward(
        unrotated_query.reshape(length, heads, HEAD_SIZE), cosine, sine_table
    ).astype(jnp.bfloat16)
    key = rotate_forward(
        unrotated_key.reshape(length, kv_heads, HEAD_SIZE), cosine, sine_table
    ).astype(jnp.bfloat16)
    value = projected_value.reshape(length, kv_heads, HEAD_SIZE).astype(jnp.bfloat16)
    query_grouped = query.reshape(length, kv_heads, group_size, HEAD_SIZE)
    upstream = upstream_flat.reshape(length, kv_heads, group_size, HEAD_SIZE)
    scale = 1.0 / jnp.sqrt(jnp.float32(HEAD_SIZE))
    scores = (
        jnp.einsum("ikgd,jkd->kgij", query_grouped, key, preferred_element_type=jnp.float32) * scale
    )
    positions = jnp.arange(length, dtype=jnp.int32)
    causal = positions[:, None] >= positions[None, :]
    scores = jnp.where(causal, scores, -jnp.inf)
    row_max = jnp.max(scores, axis=-1, keepdims=True)
    weights = jnp.exp(scores - row_max)
    weights = weights / jnp.sum(weights, axis=-1, keepdims=True)
    weights_b = weights.astype(jnp.bfloat16)
    dprob = jnp.einsum("ikgd,jkd->kgij", upstream, value, preferred_element_type=jnp.float32)
    rowdot = jnp.sum(weights * dprob, axis=-1, keepdims=True)
    dscore = (weights * (dprob - rowdot) * scale).astype(jnp.bfloat16)
    dquery = jnp.einsum("kgij,jkd->ikgd", dscore, key, preferred_element_type=jnp.float32).reshape(
        length, heads, HEAD_SIZE
    )
    dkey = jnp.einsum("kgij,ikgd->jkd", dscore, query_grouped, preferred_element_type=jnp.float32)
    dvalue = jnp.einsum("kgij,ikgd->jkd", weights_b, upstream, preferred_element_type=jnp.float32)
    query_gradient = (
        rotate_back(dquery, cosine, sine_table)
        .astype(jnp.bfloat16)
        .reshape(length, heads * HEAD_SIZE)
    )
    key_gradient = (
        rotate_back(dkey, cosine, sine_table)
        .astype(jnp.bfloat16)
        .reshape(length, kv_heads * HEAD_SIZE)
    )
    value_gradient = dvalue.astype(jnp.bfloat16).reshape(length, kv_heads * HEAD_SIZE)
    return (query_gradient, key_gradient, value_gradient)


DP_AXES = ("y", "zl", "x")
TP_AXES = ("zh", "c")


def gather_rows(block):
    block = lax.all_gather(block, "x", axis=0, tiled=True)
    block = lax.all_gather(block, "zl", axis=0, tiled=True)
    return lax.all_gather(block, "y", axis=0, tiled=True)


def scatter_rows(block):
    block = lax.psum_scatter(block, "y", scatter_dimension=0, tiled=True)
    block = lax.psum_scatter(block, "zl", scatter_dimension=0, tiled=True)
    return lax.psum_scatter(block, "x", scatter_dimension=0, tiled=True)


def body(tokens, grad_out, w_query, w_key, value_matrix):
    query_cols = w_query.shape[1]
    key_value_columns = w_key.shape[1]
    kv_dev = key_value_columns // HEAD_SIZE
    weights_all = gather_rows(jnp.concatenate([w_query, w_key, value_matrix], axis=1))
    projected = jnp.dot(tokens, weights_all, preferred_element_type=jnp.float32)
    unrotated_query = projected[:, :query_cols]
    unrotated_key = projected[:, query_cols : query_cols + key_value_columns]
    projected_value = projected[:, query_cols + key_value_columns :]
    query_gradient, key_gradient, value_gradient = attention_backward(
        unrotated_query, unrotated_key, projected_value, grad_out, kv_dev
    )
    combined = jnp.concatenate([query_gradient, key_gradient, value_gradient], axis=1)
    partial_sum = lax.dot_general(
        combined, weights_all, (((1,), (1,)), ((), ())), preferred_element_type=jnp.float32
    )
    grad_tokens = lax.psum_scatter(
        partial_sum.astype(jnp.bfloat16), TP_AXES, scatter_dimension=1, tiled=True
    )
    grads_all = scatter_rows(
        lax.dot_general(
            tokens, combined, (((0,), (0,)), ((), ())), preferred_element_type=jnp.float32
        ).astype(jnp.bfloat16)
    )
    grad_query = grads_all[:, :query_cols]
    grad_key = grads_all[:, query_cols : query_cols + key_value_columns]
    grad_value = grads_all[:, query_cols + key_value_columns :]
    return (grad_tokens, grad_query, grad_key, grad_value)


def solution(mesh):
    view = Mesh(mesh.devices.reshape(4, 2, 4, 2, 2), DP_AXES + TP_AXES)
    rows = P(DP_AXES, None)
    split = P(DP_AXES, TP_AXES)
    in_specs = (rows, split, split, split, split)
    out_specs = (split, split, split, split)
    return jax.shard_map(body, mesh=view, in_specs=in_specs, out_specs=out_specs, check_vma=False)
```

profile of v0, /device:TPU:1, one launch (start us, length us, event | category | flops | bytes accessed | tf_op | source)
XLA Modules:
  0.0 409.0 jit_solution(8105089729358219273)
XLA Ops:
  7.2 0.0 all-gather.3.cloned.1.call-start
  7.2 1.0 pad_maximum_fusion.6
  8.2 13.3 %all_gather.9 = bf16[512,768]{1,0:T(8,128)(2,1)} all-gather(bf16[128,768]{1,0:T(8,128)(2,1)S(1)} %pad_maximum_fusion.6), channel_id=1, replica_groups=mesh['y'=4,'zl'=2,'x'=4,'zh'=2,'c'=2] {'x'}, dimensions={0}, use_global_device_ids=true | all-gather | bytes 983040 | tf_op jit(solution)/shard_map/all_gather | solution.py:89
  21.5 0.0 all-gather.3.cloned.1.call-update
  21.5 0.0 all-gather.5.cloned.1.call-start
  21.6 34.3 %all-gather.3.cloned.1.call-done = bf16[1024,768]{1,0:T(8,128)(2,1)} async-done(((bf16[512,768]{1,0:T(8,128)(2,1)}), bf16[1024,768]{1,0:T(8,128)(2,1)}) %all-gather.3.cloned.1.call-update) | async-done | bytes 1572880 | tf_op jit(solution)/shard_map/all_gather | solution.py:90
  55.9 0.0 all-gather.5.cloned.1.call-update
  55.9 0.0 reduce-scatter.9.cloned.1.call-start
  55.9 2.3 copy.44
  58.2 0.3 iota_compare_fusion
  58.5 1.0 fusion.34
  59.5 64.7 %all-gather.5.cloned.1.call-done = bf16[4096,768]{1,0:T(8,128)(2,1)} async-done(((bf16[1024,768]{1,0:T(8,128)(2,1)}), bf16[4096,768]{1,0:T(8,128)(2,1)}) %all-gather.5.cloned.1.call-update) | async-done | bytes 6291472 | tf_op jit(solution)/shard_map/all_gather | solution.py:91
  124.2 11.0 %convolution_bitcast_fusion = f32[1024,768]{0,1:T(8,128)S(1)} fusion(bf16[4096,768]{1,0:T(8,128)(2,1)} %all-gather.5.cloned.1.call-done, bf16[1024,4096]{1,0:T(8,128)(2,1)} %param.5), kind=kOutput, calls=%fused_computation.29 | convolution fusion | flops 6442450944 | bytes 17825792 | tf_op jit(solution)/shard_map/dot_general | solution.py:105
  135.3 1.6 slice.26
  136.9 1.8 slice_negate_fusion.1
  138.7 0.2 pad_maximum_fusion.4
  138.9 0.3 maximum_multiply_fusion
  139.2 0.5 copy-done.5
  139.7 0.6 fusion.14
  140.3 0.7 copy-done.1
  141.0 3.1 fusion.6
  144.1 3.7 fusion.5
  147.8 0.6 copy-done.14
  148.4 6.0 %fusion.20 = bf16[1024,128]{0,1:T(8,128)(2,1)} fusion(bf16[1024,4,128]{0,2,1:T(8,128)(2,1)S(1)} %bitcast.123, f32[4,1024]{1,0:T(4,128)S(1)} %fusion.5, f32[4,1024]{1,0:T(4,128)S(1)} %get-tuple-element.27, f32[1024,1024,4]{1,0,2:T(8,128)S(1)} %get-tuple-element.28, pred[1024,1024]{0,1:T(8,128)(4,1)S(1)} %iota_compare_fusion), kind=kOutput, calls=%fused_computation.33 | convolution fusion | flops 1094844416 | bytes 19169280 | tf_op jit(solution)/shard_map/kgij,ikgd->jkd/dot_general | solution.py:69
  154.4 11.1 %fusion = (f32[4,1024]{1,0:T(4,128)}, f32[1024,1024,4]{1,0,2:T(8,128)}) fusion(f32[4,1024]{1,0:T(4,128)} %copy-done.14, f32[4,1024]{1,0:T(4,128)} %copy-done.13, f32[1024,1024,4]{1,0,2:T(8,128)S(1)} %get-tuple-element.28, pred[1024,1024]{0,1:T(8,128)(4,1)S(1)} %iota_compare_fusion, bf16[1024,4,128]{0,2,1:T(8,128)(2,1)} %bitcast.122, f32[1024,768]{0,1:T(8,128)} %copy-done.2), kind=kOutput, calls=%fused_computation.3 | convolution fusion | flops 1098903552 | bytes 35962880 | tf_op jit(solution)/shard_map/ikgd,jkd->kgij/dot_general | solution.py:62
  165.5 11.6 %fusion.7 = bf16[4,1024,1024]{1,2,0:T(8,128)(2,1)} fusion(f32[1024,1024,4]{1,0,2:T(8,128)} %get-tuple-element.30, f32[4,1024]{1,0:T(4,128)} %get-tuple-element.29, f32[4,1024]{1,0:T(4,128)} %copy-done.14, f32[4,1024]{1,0:T(4,128)} %copy-done.13, f32[1024,1024,4]{1,0,2:T(8,128)S(1)} %get-tuple-element.28, pred[1024,1024]{0,1:T(8,128)(4,1)S(1)} %iota_compare_fusion), kind=kLoop, calls=%fused_computation.11 | loop fusion | flops 33554432 | bytes 43040768 | tf_op jit(solution)/shard_map/reshape.19
  177.1 7.8 %bitcast_multiply_fusion.4 = (f32[1024,1,128]{0,2,1:T(8,128)S(1)}, f32[1024,1,128]{0,2,1:T(8,128)S(1)}) fusion(f32[1024,64]{0,1:T(8,128)} %copy-done.7, bf16[4,1024,1024]{1,2,0:T(8,128)(2,1)} %fusion.7, f32[1024,4,128]{0,2,1:T(8,128)} %copy-done.1, f32[1024,4,128]{0,2,1:T(8,128)} %bitcast.7, f32[1024,128]{0,1:T(8,128)} %copy-done.3), kind=kOutput, calls=%fused_computation.45 | convolution fusion | flops 1075576832 | bytes 14417920 | tf_op jit(solution)/shard_map/kgij,ikgd->jkd/dot_general | solution.py:68
  185.0 1.4 bitcast_multiply_fusion.3
  186.4 0.2 slice_negate_fusion
  186.6 0.2 pad_maximum_fusion
  186.9 0.5 copy-done.4
  187.4 0.6 fusion.16
  188.0 0.1 fusion.27
  188.1 0.7 slice-done
  188.8 0.0 copy-done.15
  188.9 1.3 slice-done.1
  190.2 8.7 %fusion.11 = bf16[4096,768]{0,1:T(8,128)(2,1)} fusion(bf16[1024,4096]{1,0:T(8,128)(2,1)S(1)} %bitcast.125, bf16[1024,128]{0,1:T(8,128)(2,1)S(1)} %copy-done.15, bf16[1024,128]{0,1:T(8,128)(2,1)S(1)} %fusion.27, bf16[1024,512]{0,1:T(8,128)(2,1)S(1)} %fusion.16), kind=kOutput, calls=%fused_computation.17 | convolution fusion | flops 6450315264 | bytes 16252928 | tf_op jit(solution)/shard_map/dot_general | solution.py:120
  198.9 0.0 reduce-scatter.11.cloned.1.call-start
  199.0 64.8 %reduce-scatter.9.cloned.1.call-done = bf16[1024,768]{0,1:T(8,128)(2,1)} async-done(((bf16[4096,768]{0,1:T(8,128)(2,1)}), bf16[1024,768]{0,1:T(8,128)(2,1)}) %reduce-scatter.9.cloned.1.call-update) | async-done | bytes 1572880 | tf_op jit(solution)/shard_map/reduce_scatter | solution.py:95
  263.8 0.0 reduce-scatter.13.cloned.1.call-start
  263.8 30.5 %reduce-scatter.11.cloned.1.call-done = bf16[512,768]{0,1:T(8,128)(2,1)} async-done(((bf16[1024,768]{0,1:T(8,128)(2,1)}), bf16[512,768]{0,1:T(8,128)(2,1)}) %reduce-scatter.11.cloned.1.call-update) | async-done | bytes 786448 | tf_op jit(solution)/shard_map/reduce_scatter | solution.py:96
  294.3 2.4 copy.39
  296.7 0.0 reduce-scatter.7.cloned.1.call-start
  296.8 11.8 %convolution_convert_fusion = bf16[1024,4096]{1,0:T(8,128)(2,1)} fusion(bf16[4096,768]{1,0:T(8,128)(2,1)} %all-gather.5.cloned.1.call-done, bf16[1024,128]{0,1:T(8,128)(2,1)S(1)} %copy-done.15, bf16[1024,128]{0,1:T(8,128)(2,1)S(1)} %fusion.27, bf16[1024,512]{0,1:T(8,128)(2,1)S(1)} %fusion.16), kind=kOutput, calls=%fused_computation.15 | convolution fusion | flops 6451363840 | bytes 16252928 | tf_op jit(solution)/shard_map/dot_general | solution.py:113
  308.6 10.5 %reduce-scatter.13.cloned.1.call-done = bf16[128,768]{1,0:T(8,128)(2,1)} async-done(((bf16[512,768]{1,0:T(8,128)(2,1)}), bf16[128,768]{1,0:T(8,128)(2,1)}) %reduce-scatter.13.cloned.1.call-update) | async-done | bytes 196624
  319.2 1.6 slice.28
  320.7 1.4 fusion.39
  322.2 80.0 %reduce-scatter.7.cloned.1.call-done = bf16[1024,1024]{1,0:T(8,128)(2,1)} async-done(((bf16[1024,4096]{1,0:T(8,128)(2,1)}), bf16[1024,1024]{1,0:T(8,128)(2,1)}) %reduce-scatter.7.cloned.1.call-update) | async-done | bytes 2097168 | tf_op jit(solution)/shard_map/reduce_scatter | solution.py:116
  (38 shorter events, 0.3 us)
Async XLA Ops:
  7.2 48.7 %all-gather.3.cloned.1.call-start = ((), (), s32[]{:S(2)}) async-start(), calls=%async_computation.4 | async-start | bytes 2359296 | tf_op jit(solution)/shard_map/all_gather | solution.py:90
  21.5 102.7 %all-gather.5.cloned.1.call-start = ((), (), s32[]{:S(2)}) async-start(), calls=%async_computation.5 | async-start | bytes 7864320 | tf_op jit(solution)/shard_map/all_gather | solution.py:91
  55.9 207.8 %reduce-scatter.9.cloned.1.call-start = ((), (), s32[]{:S(2)}) async-start(), calls=%async_computation.7 | async-start | bytes 7864320 | tf_op jit(solution)/shard_map/reduce_scatter | solution.py:95
  59.5 79.2 %copy-start.7 = (f32[1024,64]{0,1:T(8,128)}, f32[1024,64]{0,1:T(8,128)S(1)}, u32[]{:S(2)}) copy-start(f32[1024,64]{0,1:T(8,128)S(1)} %get-tuple-element.26) | copy-start | bytes 786436
  59.5 79.2 %copy-start.10 = (f32[1024,64]{0,1:T(8,128)}, f32[1024,64]{0,1:T(8,128)S(1)}, u32[]{:S(2)}) copy-start(f32[1024,64]{0,1:T(8,128)S(1)} %get-tuple-element.25) | copy-start | bytes 786436
  135.2 4.4 %copy-start.2 = (f32[1024,768]{0,1:T(8,128)}, f32[1024,768]{0,1:T(8,128)S(1)}, u32[]{:S(2)}) copy-start(f32[1024,768]{0,1:T(8,128)S(1)} %convolution_bitcast_fusion) | copy-start | bytes 9437188
  138.9 0.8 copy-start.5
  138.9 1.4 copy-start.3
  138.9 5.2 %copy-start.8 = (bf16[1024,128,1]{0,1,2:T(8,128)(2,1)}, bf16[1024,128,1]{0,1,2:T(8,128)(2,1)S(1)}, u32[]{:S(2)}) copy-start(bf16[1024,128,1]{0,1,2:T(8,128)(2,1)S(1)} %get-tuple-element.21) | copy-start | bytes 786436
  139.7 1.3 copy-start.1
  144.1 3.7 copy-start.13
  144.1 4.3 %copy-start.12 = (bf16[1024,512]{0,1:T(8,128)(2,1)S(1)}, bf16[1024,512]{0,1:T(8,128)(2,1)}, u32[]{:S(2)}) copy-start(bf16[1024,512]{0,1:T(8,128)(2,1)} %copy.44) | copy-start | bytes 3145732
  147.8 0.6 copy-start.14
  177.1 7.9 %copy-start = (bf16[4,1024,1024]{1,2,0:T(8,128)(2,1)S(1)}, bf16[4,1024,1024]{1,2,0:T(8,128)(2,1)}, u32[]{:S(2)}) copy-start(bf16[4,1024,1024]{1,2,0:T(8,128)(2,1)} %fusion.7) | copy-start | bytes 25165828
  177.1 7.9 %copy-start.6 = (f32[1024,128]{0,1:T(8,128)S(1)}, f32[1024,128]{0,1:T(8,128)}, u32[]{:S(2)}) copy-start(f32[1024,128]{0,1:T(8,128)} %copy-done.5) | copy-start | bytes 1572868
  177.1 7.9 %copy-start.9 = (bf16[1024,128,1]{0,1,2:T(8,128)(2,1)S(1)}, bf16[1024,128,1]{0,1,2:T(8,128)(2,1)}, u32[]{:S(2)}) copy-start(bf16[1024,128,1]{0,1,2:T(8,128)(2,1)} %copy-done.8) | copy-start | bytes 786436
  186.4 1.0 copy-start.4
  186.4 1.6 copy-start.11
  186.4 2.4 slice-start
  186.6 2.3 copy-start.15
  186.6 3.6 slice-start.1
  198.9 95.4 %reduce-scatter.11.cloned.1.call-start = ((), (), s32[]{:S(2)}) async-start(), calls=%async_computation.8 | async-start | bytes 2359296 | tf_op jit(solution)/shard_map/reduce_scatter | solution.py:96
  263.8 55.4 %reduce-scatter.13.cloned.1.call-start = ((), (), s32[]{:S(2)}) async-start(), calls=%async_computation.9 | async-start | bytes 983040
  296.7 105.4 %reduce-scatter.7.cloned.1.call-start = ((), (), s32[]{:S(2)}) async-start(), calls=%async_computation.6 | async-start | bytes 10485760 | tf_op jit(solution)/shard_map/reduce_scatter | solution.py:116
Sparse Core Ops, SparseCore 0:
  21.6 34.1 all-gather.2
  57.5 66.6 all-gather.4
  199.0 64.6 reduce-scatter.8
  265.9 28.3 reduce-scatter.10
  296.8 22.2 reduce-scatter.12
  322.5 79.5 reduce-scatter.6
where the time goes:
time: 409 us
  waiting for transfers between devices  285 us (70%)
  matrix products  60.9 us (15%)
  other arithmetic  21.5 us (5%)
  between operations  14.4 us (4%)
  local copies, waits for them, and re-layouts  13.7 us (3%)
  blocking collectives  13.3 us (3%)
    reduce_scatter x1, waiting for transfers between devices, body(): lax.psum_scatter(partial_sum.astype(jnp.bfloat16), TP_AXES, scatter_dimen...  80 us
    reduce_scatter x1, waiting for transfers between devices, scatter_rows(): block = lax.psum_scatter(block, 'y', scatter_dimension=0, tiled=True)  64.8 us
    all_gather x1, waiting for transfers between devices, gather_rows(): return lax.all_gather(block, 'y', axis=0, tiled=True)  64.7 us
    all_gather x1, waiting for transfers between devices, gather_rows(): block = lax.all_gather(block, 'zl', axis=0, tiled=True)  34.3 us
    reduce_scatter x1, waiting for transfers between devices, scatter_rows(): block = lax.psum_scatter(block, 'zl', scatter_dimension=0, tiled=True)  30.5 us
    all_gather x1, blocking collectives, gather_rows(): block = lax.all_gather(block, 'x', axis=0, tiled=True)  13.3 us
    dot_general x1, matrix products, body(): lax.dot_general(combined, weights_all, (((1,), (1,)), ((), ())), preferre...  11.8 us
    another operation x1, other arithmetic  11.6 us
  transfers between devices with their start and end apart: 6, of which 6 were waited for; matrix products, arithmetic and copies ran while one was open for 4% of the time, Pallas kernels for 0%

commit v1 on v0

--- a/solution.py
+++ b/solution.py
@@ -87,7 +87,9 @@
 
 def gather_rows(block):
     block = lax.all_gather(block, "x", axis=0, tiled=True)
-    block = lax.all_gather(block, "zl", axis=0, tiled=True)
+    block = jnp.concatenate(
+        lax.all_to_all(jnp.stack([block] * lax.axis_size("zl")), "zl", 0, 0), axis=0
+    )
     return lax.all_gather(block, "y", axis=0, tiled=True)
 
 

time: 409 us -> 396 us (0.968)
  waiting for transfers between devices: 285 us -> 252 us
  blocking collectives: 13.3 us -> 33.7 us
    all_gather x1 -> x0, waiting for transfers between devices: 34.3 us -> none  [gather_rows(): block = lax.all_gather(block, 'zl', axis=0, tiled=True)]
    all_to_all x0 -> x1, blocking collectives: none -> 20.8 us  [gather_rows(): lax.all_to_all(jnp.stack([block] * lax.axis_size('zl')), 'zl', 0, 0)]
    another operation x1 -> x2, other arithmetic: 11.6 us -> 11.7 us
    unnamed x7 -> x6, waiting for transfers between devices: 10.6 us -> 10.6 us
  transfers between devices with their start and end apart: 6 -> 5, of which waited for: 6 -> 5; matrix products, arithmetic and copies ran while one was open for 4% -> 4% of each run, Pallas kernels for 0% -> 0%
where the time goes in v1:
time: 396 us; the launch traced here: 395 us
  waiting for transfers between devices  252 us (64%)
  matrix products  60.9 us (15%)
  blocking collectives  33.7 us (9%)
  other arithmetic  21.7 us (5%)
  between operations  14.1 us (4%)
  local copies, waits for them, and re-layouts  12.7 us (3%)
    reduce_scatter x1, waiting for transfers between devices, body(): lax.psum_scatter(partial_sum.astype(jnp.bfloat16), TP_AXES, scatter_dimen...  80 us
    all_gather x1, waiting for transfers between devices, gather_rows(): return lax.all_gather(block, 'y', axis=0, tiled=True)  66 us
    reduce_scatter x1, waiting for transfers between devices, scatter_rows(): block = lax.psum_scatter(block, 'y', scatter_dimension=0, tiled=True)  64.8 us
    reduce_scatter x1, waiting for transfers between devices, scatter_rows(): block = lax.psum_scatter(block, 'zl', scatter_dimension=0, tiled=True)  30.6 us
    all_to_all x1, blocking collectives, gather_rows(): lax.all_to_all(jnp.stack([block] * lax.axis_size('zl')), 'zl', 0, 0)  20.8 us
    all_gather x1, blocking collectives, gather_rows(): block = lax.all_gather(block, 'x', axis=0, tiled=True)  12.9 us
    dot_general x1, matrix products, body(): lax.dot_general(combined, weights_all, (((1,), (1,)), ((), ())), preferre...  11.8 us
    another operation x1, other arithmetic  11.6 us
  transfers between devices with their start and end apart: 5, of which 5 were waited for; matrix products, arithmetic and copies ran while one was open for 4% of the time, Pallas kernels for 0%

profile of v1, /device:TPU:1, one launch (start us, length us, event | category | flops | bytes accessed | tf_op | source)
XLA Modules:
  0.0 395.5 jit_solution(3762333005702257613)
XLA Ops:
  7.2 0.0 all-gather.2.cloned.1.call-start
  7.2 1.0 pad_maximum_fusion.7
  8.3 12.9 %all_gather.6 = bf16[512,768]{1,0:T(8,128)(2,1)S(1)} all-gather(bf16[128,768]{1,0:T(8,128)(2,1)S(1)} %pad_maximum_fusion.7), channel_id=1, replica_groups=mesh['y'=4,'zl'=2,'x'=4,'zh'=2,'c'=2] {'x'}, dimensions={0}, use_global_device_ids=true | all-gather | bytes 983040 | tf_op jit(solution)/shard_map/all_gather | solution.py:89
  21.2 0.1 pad_maximum_fusion.1
  21.3 20.8 %all_to_all.5 = bf16[2,512,768]{2,1,0:T(8,128)(2,1)} all-to-all(bf16[2,512,768]{2,1,0:T(8,128)(2,1)S(1)} %pad_maximum_fusion.1), channel_id=1, replica_groups=mesh['y'=4,'zl'=2,'x'=4,'zh'=2,'c'=2] {'zl'}, dimensions={0} | all-to-all | bytes 3145728 | tf_op jit(solution)/shard_map/all_to_all | solution.py:91
  42.2 0.0 all-gather.2.cloned.1.call-update
  42.2 0.0 reduce-scatter.9.cloned.1.call-start
  42.2 1.3 copy.44
  43.5 0.3 iota_compare_fusion
  43.9 1.0 fusion.34
  44.9 66.0 %all-gather.2.cloned.1.call-done = bf16[4096,768]{1,0:T(8,128)(2,1)} async-done(((bf16[1024,768]{1,0:T(8,128)(2,1)}), bf16[4096,768]{1,0:T(8,128)(2,1)}) %all-gather.2.cloned.1.call-update) | async-done | bytes 6291472 | tf_op jit(solution)/shard_map/all_gather | solution.py:93
  110.9 11.0 %convolution_bitcast_fusion = f32[1024,768]{0,1:T(8,128)S(1)} fusion(bf16[4096,768]{1,0:T(8,128)(2,1)} %all-gather.2.cloned.1.call-done, bf16[1024,4096]{1,0:T(8,128)(2,1)} %param.5), kind=kOutput, calls=%fused_computation.29 | convolution fusion | flops 6442450944 | bytes 17825792 | tf_op jit(solution)/shard_map/dot_general | solution.py:107
  122.0 1.6 slice.26
  123.6 1.7 slice_negate_fusion.1
  125.4 0.2 pad_maximum_fusion.5
  125.6 0.3 maximum_multiply_fusion
  125.9 0.5 copy-done.5
  126.4 0.6 fusion.14
  126.9 0.7 copy-done.1
  127.7 3.1 fusion.6
  130.8 3.7 fusion.5
  134.5 0.6 copy-done.15
  135.1 6.0 %fusion.20 = bf16[1024,128]{0,1:T(8,128)(2,1)} fusion(bf16[1024,4,128]{0,2,1:T(8,128)(2,1)S(1)} %bitcast.127, f32[4,1024]{1,0:T(4,128)S(1)} %fusion.5, f32[4,1024]{1,0:T(4,128)S(1)} %get-tuple-element.27, f32[1024,1024,4]{1,0,2:T(8,128)S(1)} %get-tuple-element.28, pred[1024,1024]{0,1:T(8,128)(4,1)S(1)} %iota_compare_fusion), kind=kOutput, calls=%fused_computation.34 | convolution fusion | flops 1094844416 | bytes 19169280 | tf_op jit(solution)/shard_map/kgij,ikgd->jkd/dot_general | solution.py:69
  141.1 11.1 %fusion = (f32[4,1024]{1,0:T(4,128)}, f32[1024,1024,4]{1,0,2:T(8,128)}) fusion(f32[4,1024]{1,0:T(4,128)} %copy-done.15, f32[4,1024]{1,0:T(4,128)} %copy-done.14, f32[1024,1024,4]{1,0,2:T(8,128)S(1)} %get-tuple-element.28, pred[1024,1024]{0,1:T(8,128)(4,1)S(1)} %iota_compare_fusion, bf16[1024,4,128]{0,2,1:T(8,128)(2,1)} %bitcast.126, f32[1024,768]{0,1:T(8,128)} %copy-done.2), kind=kOutput, calls=%fused_computation.3 | convolution fusion | flops 1098903552 | bytes 35962880 | tf_op jit(solution)/shard_map/ikgd,jkd->kgij/dot_general | solution.py:62
  152.2 11.6 %fusion.7 = bf16[4,1024,1024]{1,2,0:T(8,128)(2,1)} fusion(f32[1024,1024,4]{1,0,2:T(8,128)} %get-tuple-element.30, f32[4,1024]{1,0:T(4,128)} %get-tuple-element.29, f32[4,1024]{1,0:T(4,128)} %copy-done.15, f32[4,1024]{1,0:T(4,128)} %copy-done.14, f32[1024,1024,4]{1,0,2:T(8,128)S(1)} %get-tuple-element.28, pred[1024,1024]{0,1:T(8,128)(4,1)S(1)} %iota_compare_fusion), kind=kLoop, calls=%fused_computation.11 | loop fusion | flops 33554432 | bytes 43040768 | tf_op jit(solution)/shard_map/reshape.20
  163.8 7.8 %bitcast_multiply_fusion.4 = (f32[1024,1,128]{0,2,1:T(8,128)S(1)}, f32[1024,1,128]{0,2,1:T(8,128)S(1)}) fusion(f32[1024,64]{0,1:T(8,128)} %copy-done.7, bf16[4,1024,1024]{1,2,0:T(8,128)(2,1)} %fusion.7, f32[1024,4,128]{0,2,1:T(8,128)} %copy-done.1, f32[1024,4,128]{0,2,1:T(8,128)} %bitcast.9, f32[1024,128]{0,1:T(8,128)} %copy-done.3), kind=kOutput, calls=%fused_computation.46 | convolution fusion | flops 1075576832 | bytes 14417920 | tf_op jit(solution)/shard_map/kgij,ikgd->jkd/dot_general | solution.py:68
  171.6 1.4 bitcast_multiply_fusion.3
  173.1 0.2 slice_negate_fusion
  173.3 0.2 pad_maximum_fusion
  173.5 0.5 copy-done.4
  174.1 0.6 fusion.16
  174.7 0.1 fusion.27
  174.8 0.7 slice-done
  175.5 0.0 copy-done.16
  175.5 1.3 slice-done.1
  176.8 8.7 %fusion.11 = bf16[4096,768]{0,1:T(8,128)(2,1)} fusion(bf16[1024,4096]{1,0:T(8,128)(2,1)S(1)} %bitcast.129, bf16[1024,128]{0,1:T(8,128)(2,1)S(1)} %copy-done.16, bf16[1024,128]{0,1:T(8,128)(2,1)S(1)} %fusion.27, bf16[1024,512]{0,1:T(8,128)(2,1)S(1)} %fusion.16), kind=kOutput, calls=%fused_computation.17 | convolution fusion | flops 6450315264 | bytes 16252928 | tf_op jit(solution)/shard_map/dot_general | solution.py:122
  185.5 0.0 reduce-scatter.9.cloned.1.call-update
  185.5 0.0 reduce-scatter.11.cloned.1.call-start
  185.6 64.8 %reduce-scatter.9.cloned.1.call-done = bf16[1024,768]{0,1:T(8,128)(2,1)} async-done(((bf16[4096,768]{0,1:T(8,128)(2,1)}), bf16[1024,768]{0,1:T(8,128)(2,1)}) %reduce-scatter.9.cloned.1.call-update) | async-done | bytes 1572880 | tf_op jit(solution)/shard_map/reduce_scatter | solution.py:97
  250.4 0.0 reduce-scatter.13.cloned.1.call-start
  250.5 30.6 %reduce-scatter.11.cloned.1.call-done = bf16[512,768]{0,1:T(8,128)(2,1)} async-done(((bf16[1024,768]{0,1:T(8,128)(2,1)}), bf16[512,768]{0,1:T(8,128)(2,1)}) %reduce-scatter.11.cloned.1.call-update) | async-done | bytes 786448 | tf_op jit(solution)/shard_map/reduce_scatter | solution.py:98
  281.1 2.4 copy.39
  283.5 0.0 reduce-scatter.7.cloned.1.call-start
  283.6 11.8 %convolution_convert_fusion = bf16[1024,4096]{1,0:T(8,128)(2,1)} fusion(bf16[4096,768]{1,0:T(8,128)(2,1)} %all-gather.2.cloned.1.call-done, bf16[1024,128]{0,1:T(8,128)(2,1)S(1)} %copy-done.16, bf16[1024,128]{0,1:T(8,128)(2,1)S(1)} %fusion.27, bf16[1024,512]{0,1:T(8,128)(2,1)S(1)} %fusion.16), kind=kOutput, calls=%fused_computation.15 | convolution fusion | flops 6451363840 | bytes 16252928 | tf_op jit(solution)/shard_map/dot_general | solution.py:115
  295.4 10.6 %reduce-scatter.13.cloned.1.call-done = bf16[128,768]{1,0:T(8,128)(2,1)} async-done(((bf16[512,768]{1,0:T(8,128)(2,1)}), bf16[128,768]{1,0:T(8,128)(2,1)}) %reduce-scatter.13.cloned.1.call-update) | async-done | bytes 196624
  306.0 1.6 slice.28
  307.5 1.4 fusion.39
  308.9 80.0 %reduce-scatter.7.cloned.1.call-done = bf16[1024,1024]{1,0:T(8,128)(2,1)} async-done(((bf16[1024,4096]{1,0:T(8,128)(2,1)}), bf16[1024,1024]{1,0:T(8,128)(2,1)}) %reduce-scatter.7.cloned.1.call-update) | async-done | bytes 2097168 | tf_op jit(solution)/shard_map/reduce_scatter | solution.py:118
  (39 shorter events, 0.3 us)
Async XLA Ops:
  7.2 35.1 %copy-start.12 = (bf16[1024,512]{1,0:T(8,128)(2,1)S(1)}, bf16[1024,512]{1,0:T(8,128)(2,1)}, u32[]{:S(2)}) copy-start(bf16[1024,512]{1,0:T(8,128)(2,1)} %param.6) | copy-start | bytes 3145732
  7.2 103.7 %all-gather.2.cloned.1.call-start = ((), (), s32[]{:S(2)}) async-start(), calls=%async_computation.5 | async-start | bytes 7864320 | tf_op jit(solution)/shard_map/all_gather | solution.py:93
  42.2 208.2 %reduce-scatter.9.cloned.1.call-start = ((), (), s32[]{:S(2)}) async-start(), calls=%async_computation.7 | async-start | bytes 7864320 | tf_op jit(solution)/shard_map/reduce_scatter | solution.py:97
  44.9 80.5 %copy-start.7 = (f32[1024,64]{0,1:T(8,128)}, f32[1024,64]{0,1:T(8,128)S(1)}, u32[]{:S(2)}) copy-start(f32[1024,64]{0,1:T(8,128)S(1)} %get-tuple-element.26) | copy-start | bytes 786436
  44.9 80.5 %copy-start.10 = (f32[1024,64]{0,1:T(8,128)}, f32[1024,64]{0,1:T(8,128)S(1)}, u32[]{:S(2)}) copy-start(f32[1024,64]{0,1:T(8,128)S(1)} %get-tuple-element.25) | copy-start | bytes 786436
  121.9 4.4 %copy-start.2 = (f32[1024,768]{0,1:T(8,128)}, f32[1024,768]{0,1:T(8,128)S(1)}, u32[]{:S(2)}) copy-start(f32[1024,768]{0,1:T(8,128)S(1)} %convolution_bitcast_fusion) | copy-start | bytes 9437188
  125.6 0.8 copy-start.5
  125.6 1.4 copy-start.3
  125.6 5.2 %copy-start.8 = (bf16[1024,128,1]{0,1,2:T(8,128)(2,1)}, bf16[1024,128,1]{0,1,2:T(8,128)(2,1)S(1)}, u32[]{:S(2)}) copy-start(bf16[1024,128,1]{0,1,2:T(8,128)(2,1)S(1)} %get-tuple-element.21) | copy-start | bytes 786436
  126.4 1.3 copy-start.1
  130.8 3.7 copy-start.14
  130.8 4.3 %copy-start.13 = (bf16[1024,512]{0,1:T(8,128)(2,1)S(1)}, bf16[1024,512]{0,1:T(8,128)(2,1)}, u32[]{:S(2)}) copy-start(bf16[1024,512]{0,1:T(8,128)(2,1)} %copy.44) | copy-start | bytes 3145732
  134.5 0.6 copy-start.15
  163.8 7.8 %copy-start = (bf16[4,1024,1024]{1,2,0:T(8,128)(2,1)S(1)}, bf16[4,1024,1024]{1,2,0:T(8,128)(2,1)}, u32[]{:S(2)}) copy-start(bf16[4,1024,1024]{1,2,0:T(8,128)(2,1)} %fusion.7) | copy-start | bytes 25165828
  163.8 7.9 %copy-start.6 = (f32[1024,128]{0,1:T(8,128)S(1)}, f32[1024,128]{0,1:T(8,128)}, u32[]{:S(2)}) copy-start(f32[1024,128]{0,1:T(8,128)} %copy-done.5) | copy-start | bytes 1572868
  163.8 7.9 %copy-start.9 = (bf16[1024,128,1]{0,1,2:T(8,128)(2,1)S(1)}, bf16[1024,128,1]{0,1,2:T(8,128)(2,1)}, u32[]{:S(2)}) copy-start(bf16[1024,128,1]{0,1,2:T(8,128)(2,1)} %copy-done.8) | copy-start | bytes 786436
  173.0 1.0 copy-start.4
  173.1 1.6 copy-start.11
  173.1 2.4 slice-start
  173.3 2.3 copy-start.16
  173.3 3.6 slice-start.1
  185.5 95.6 %reduce-scatter.11.cloned.1.call-start = ((), (), s32[]{:S(2)}) async-start(), calls=%async_computation.8 | async-start | bytes 2359296 | tf_op jit(solution)/shard_map/reduce_scatter | solution.py:98
  250.4 55.6 %reduce-scatter.13.cloned.1.call-start = ((), (), s32[]{:S(2)}) async-start(), calls=%async_computation.9 | async-start | bytes 983040
  283.5 105.4 %reduce-scatter.7.cloned.1.call-start = ((), (), s32[]{:S(2)}) async-start(), calls=%async_computation.6 | async-start | bytes 10485760 | tf_op jit(solution)/shard_map/reduce_scatter | solution.py:118
Sparse Core Ops, SparseCore 0:
  42.3 68.5 all-gather.1
  185.7 64.6 reduce-scatter.8
  252.7 28.3 reduce-scatter.10
  283.6 22.2 reduce-scatter.12
  309.3 79.5 reduce-scatter.6
